TPU v7x, 512 devices: a whole 4x4x16 slice. The times are simulated.
512 devices in a mesh: tensor: 32 (over z_hi, x, core), seq: 16 (over z_lo, y).
Axes of the slice: x: 4, y: 4, z: 16 (z_hi: 4, z_lo: 4; z = z_hi * 4 + z_lo), core: 2. Of those that a mesh axis runs over, the one named last changes fastest.
Arguments:
- resid: bfloat16 [16, 512, 2048], P('seq', 'tensor'), may hold values from -6 to 6
- norm_gain: bfloat16 [2048], replicated, may hold values from 0.099609375 to 1.8984375
- gate_weight_matrix: bfloat16 [2048, 10944], P(None, 'tensor'), may hold values from -0.125 to 0.125
- up_weight: bfloat16 [2048, 10944], P(None, 'tensor'), may hold values from -0.125 to 0.125
- w_down: bfloat16 [10944, 2048], P('tensor'), may hold values from -0.0546875 to 0.0546875
- gate_a: bfloat16 [64, 2048, 16], P('seq', 'tensor'), may hold values from -0.125 to 0.125
- gate_b: bfloat16 [64, 16, 10944], P('seq', None, 'tensor'), may hold values from -1.5 to 1.5
- up_a: bfloat16 [64, 2048, 16], P('seq', 'tensor'), may hold values from -0.125 to 0.125
- up_b: bfloat16 [64, 16, 10944], P('seq', None, 'tensor'), may hold values from -1.5 to 1.5
- down_a: bfloat16 [64, 10944, 16], P('seq', 'tensor'), may hold values from -0.0546875 to 0.0546875
- down_b: bfloat16 [64, 16, 2048], P('seq'), may hold values from -1.5 to 1.5
- prompt_lengths: int32 [16, 8], P('seq'), may hold values from 1 to 256, 512 in all within a row
- prompt_choice: int32 [16, 8], P('seq'), may hold values from 0 to 15
- used_adapters: int32 [16], replicated, may hold values from 0 to 63, as said below
- adapter_holder: int32 [64], replicated, may hold values from 0 to 63, each once
Outputs:
- output: bfloat16 [16, 512, 2048], P('seq', 'tensor')
Inputs may be any that keep to these rules, and one draw needn't show every extreme that they name: `used_adapters`: 16 distinct adapter ids.
All inputs are finite; a program needn't handle non-finite values.
Results may differ from a plain program's by a relative error of at most 0.017.
Values may be sent and summed in bfloat16 or wider, within the bound.
No kernel may reach another device: no remote copies, remote signals or barrier semaphores. Data moves between devices by JAX's collectives and lax.ppermute only.
A program may use at most 128 MiB of HBM per device.

v0:
```python
import jax
import jax.numpy as jnp
from jax import lax
from jax.sharding import PartitionSpec as P

adapter_scale = 0.5


def choose(picker, stacked):
    flat = stacked.reshape(stacked.shape[0], -1)
    chosen = jnp.dot(picker, flat, preferred_element_type=jnp.float32).astype(jnp.bfloat16)
    return chosen.reshape((picker.shape[0],) + stacked.shape[1:])


def to_columns(stacked):
    used_n, inner, rank_n = stacked.shape
    return jnp.transpose(stacked, (1, 0, 2)).reshape(inner, used_n * rank_n)


def local(
    resid,
    norm_gain,
    gate_weight_matrix,
    up_weight,
    w_down,
    gate_a,
    gate_b,
    up_a,
    up_b,
    down_a,
    down_b,
    prompt_lengths,
    prompt_choice,
    used_adapters,
    adapter_holder,
):
    tensor_n = lax.axis_size("tensor")
    tok_dev = resid.shape[1]
    group_tok = tok_dev * tensor_n
    used_n = used_adapters.shape[0]
    rank_n = gate_a.shape[2]
    feat_loc = gate_a.shape[1]
    hidden_local = gate_weight_matrix.shape[1]
    adapters_n = adapter_holder.shape[0]
    matches = used_adapters[:, None] == jnp.arange(adapters_n, dtype=jnp.int32)[None, :]
    slot_used = jnp.sum(jnp.where(matches, adapter_holder[None, :], 0), axis=1)
    whole = (
        lax.all_gather(gate_a, "seq", axis=0, tiled=True),
        lax.all_gather(up_a, "seq", axis=0, tiled=True),
        lax.all_gather(gate_b, "seq", axis=0, tiled=True),
        lax.all_gather(up_b, "seq", axis=0, tiled=True),
        lax.all_gather(down_a, "seq", axis=0, tiled=True),
        lax.all_gather(down_b, "seq", axis=0, tiled=True),
    )
    picker = (slot_used[:, None] == jnp.arange(adapters_n, dtype=jnp.int32)[None, :]).astype(
        jnp.bfloat16
    )
    fetched = tuple((choose(picker, stacked) for stacked in whole))
    fetch_ga, fetch_ua, fetch_gb, fetch_ub, fetch_da, fetch_db = fetched
    prompt_ends = jnp.cumsum(prompt_lengths[0])
    positions = jnp.arange(group_tok, dtype=jnp.int32)
    prompt_index = jnp.sum((positions[:, None] >= prompt_ends[None, :]).astype(jnp.int32), axis=1)
    prompts_n = prompt_lengths.shape[1]
    hits = prompt_index[:, None] == jnp.arange(prompts_n, dtype=jnp.int32)[None, :]
    tok_choice = jnp.sum(jnp.where(hits, prompt_choice[0][None, :], 0), axis=1)
    token_weights = (tok_choice[:, None] == jnp.arange(used_n, dtype=jnp.int32)[None, :]).astype(
        jnp.float32
    )
    row_first = lax.axis_index("tensor") * tok_dev
    own_weights = lax.dynamic_slice_in_dim(token_weights, row_first, tok_dev, 0)
    residual_float = resid[0].astype(jnp.float32)
    scale = lax.rsqrt(jnp.mean(residual_float * residual_float, axis=-1, keepdims=True) + 1e-06)
    normalized_input = (residual_float * scale * norm_gain.astype(jnp.float32)).astype(jnp.bfloat16)
    both_in = jnp.concatenate([to_columns(fetch_ga), to_columns(fetch_ua)], axis=1)
    col_first = lax.axis_index("tensor") * feat_loc
    piece = lax.all_gather(normalized_input, "tensor", axis=0, tiled=True)
    gate_part = jnp.dot(piece, gate_weight_matrix, preferred_element_type=jnp.float32)
    up_part = jnp.dot(piece, up_weight, preferred_element_type=jnp.float32)
    own_cols = lax.dynamic_slice_in_dim(piece, col_first, feat_loc, 1)
    low_part = jnp.dot(own_cols, both_in, preferred_element_type=jnp.float32)
    joined = jnp.concatenate([gate_part, up_part, low_part], axis=1)
    plain_output = joined[:, : 2 * hidden_local]
    low_rank = joined[:, 2 * hidden_local :].reshape(group_tok, 2, used_n, rank_n)
    partial_mid = jnp.sum(low_rank * token_weights[:, None, :, None], axis=2)
    mids = lax.psum(partial_mid.astype(jnp.bfloat16), "tensor")
    weights_bf = token_weights.astype(jnp.bfloat16)
    spread = (mids[:, :, None, :] * weights_bf[:, None, :, None]).reshape(
        group_tok, 2, used_n * rank_n
    )
    gate_adapter_rows = jnp.dot(
        spread[:, 0],
        fetch_gb.reshape(used_n * rank_n, hidden_local),
        preferred_element_type=jnp.float32,
    )
    up_adapter_rows = jnp.dot(
        spread[:, 1],
        fetch_ub.reshape(used_n * rank_n, hidden_local),
        preferred_element_type=jnp.float32,
    )
    gate_preactivation = plain_output[:, :hidden_local] + adapter_scale * gate_adapter_rows
    up_preactivation = plain_output[:, hidden_local:] + adapter_scale * up_adapter_rows
    hidden = (jax.nn.silu(gate_preactivation) * up_preactivation).astype(jnp.bfloat16)
    down_total_sum = lax.psum_scatter(
        jnp.dot(hidden, w_down, preferred_element_type=jnp.float32).astype(jnp.bfloat16),
        "tensor",
        scatter_dimension=0,
        tiled=True,
    ).astype(jnp.float32)
    down_adapter_rows = jnp.dot(
        hidden, to_columns(fetch_da), preferred_element_type=jnp.float32
    ).reshape(group_tok, used_n, rank_n)
    partial_down = jnp.sum(down_adapter_rows * token_weights[:, :, None], axis=1)
    mid_down = lax.psum_scatter(
        partial_down.astype(jnp.bfloat16), "tensor", scatter_dimension=0, tiled=True
    )
    spread_down = (mid_down[:, None, :] * own_weights.astype(jnp.bfloat16)[:, :, None]).reshape(
        tok_dev, used_n * rank_n
    )
    adapter_down_term = jnp.dot(
        spread_down,
        fetch_db.reshape(used_n * rank_n, fetch_db.shape[2]),
        preferred_element_type=jnp.float32,
    )
    return (residual_float + down_total_sum + adapter_scale * adapter_down_term).astype(
        jnp.bfloat16
    )[None]


def solution(mesh):
    placed = (
        P("seq", "tensor", None),
        P(),
        P(None, "tensor"),
        P(None, "tensor"),
        P("tensor", None),
        P("seq", "tensor", None),
        P("seq", None, "tensor"),
        P("seq", "tensor", None),
        P("seq", None, "tensor"),
        P("seq", "tensor", None),
        P("seq", None, None),
        P("seq", None),
        P("seq", None),
        P(),
        P(),
    )
    return jax.shard_map(
        local, mesh=mesh, in_specs=placed, out_specs=P("seq", "tensor", None), check_vma=False
    )
```

profile of v0, /device:TPU:8, one launch (start us, length us, event | category | flops | bytes accessed | tf_op | source)
XLA Modules:
  0.0 651.8 jit_solution(14810793064661548938)
XLA Ops:
  7.4 1.1 fusion.10
  8.5 0.7 convert_element_type.78
  9.2 1.5 fusion.12
  10.8 1.3 reduce-window.8
  12.1 44.3 %all_gather.22 = bf16[64,64,16]{1,2,0:T(8,128)(2,1)S(1)} all-gather(bf16[4,64,16]{1,2,0:T(8,128)(2,1)} %param.20), channel_id=1, replica_groups=mesh['tensor'=32,'seq'=16] {'seq'}, dimensions={0}, use_global_device_ids=true | all-gather | bytes 139264 | tf_op jit(solution)/shard_map/all_gather | solution.py:48
  56.4 0.4 copy.47
  56.8 0.9 select_reduce_fusion.1
  58.3 44.6 %all_gather.23 = bf16[64,64,16]{1,2,0:T(8,128)(2,1)S(1)} all-gather(bf16[4,64,16]{1,2,0:T(8,128)(2,1)} %param.22), channel_id=1, replica_groups=mesh['tensor'=32,'seq'=16] {'seq'}, dimensions={0}, use_global_device_ids=true | all-gather | bytes 139264 | tf_op jit(solution)/shard_map/all_gather | solution.py:49
  103.9 40.5 %all_gather.24 = bf16[64,16,342]{2,1,0:T(8,128)(2,1)S(1)} all-gather(bf16[4,16,342]{2,1,0:T(8,128)(2,1)S(1)} %copy-done.2), channel_id=1, replica_groups=mesh['tensor'=32,'seq'=16] {'seq'}, dimensions={0}, use_global_device_ids=true | all-gather | bytes 744192 | tf_op jit(solution)/shard_map/all_gather | solution.py:50
  144.4 0.7 reshape.166
  145.7 44.4 %all_gather.25 = bf16[64,16,342]{2,1,0:T(8,128)(2,1)S(1)} all-gather(bf16[4,16,342]{2,1,0:T(8,128)(2,1)S(1)} %copy-done.3), channel_id=1, replica_groups=mesh['tensor'=32,'seq'=16] {'seq'}, dimensions={0}, use_global_device_ids=true | all-gather | bytes 744192 | tf_op jit(solution)/shard_map/all_gather | solution.py:51
  190.1 0.7 reshape.167
  191.1 1.0 reshape_reshape.10
  192.1 43.4 %all_gather.26 = bf16[64,342,16]{1,2,0:T(8,128)(2,1)} all-gather(bf16[4,342,16]{1,2,0:T(8,128)(2,1)S(1)} %copy-done.4), channel_id=1, replica_groups=mesh['tensor'=32,'seq'=16] {'seq'}, dimensions={0}, use_global_device_ids=true | all-gather | bytes 744192 | tf_op jit(solution)/shard_map/all_gather | solution.py:52
  235.6 2.4 copy.53
  238.0 0.5 convolution_convert_fusion.1
  238.5 1.1 reshape.169
  239.6 0.6 copy.54
  240.5 1.4 fusion.13
  242.0 167.8 %psum.7 = bf16[512,2,16]{0,2,1:T(8,128)(2,1)S(1)} all-reduce(bf16[512,2,16]{0,2,1:T(8,128)(2,1)S(1)} %multiply_reduce_fusion), channel_id=1, replica_groups=mesh['tensor'=32,'seq'=16] {'tensor'}, use_global_device_ids=true, to_apply=%region_6.7 | all-reduce | flops 16384 | bytes 65536 | tf_op jit(solution)/shard_map/psum | solution.py:85
  409.9 2.7 fusion.28
  412.9 0.9 fusion.29
  414.6 0.8 copy.57
  415.4 0.5 all-gather.5.cloned.1.call-update
  416.1 2.6 convolution_convert_fusion.4
  419.0 103.0 %reduce-scatter.7.cloned.1.call-done = bf16[16,16]{1,0:T(8,128)(2,1)} async-done(((bf16[512,16]{1,0:T(8,128)(2,1)}), bf16[16,16]{1,0:T(8,128)(2,1)}) %reduce-scatter.7.cloned.1.call-update) | async-done | bytes 528 | tf_op jit(solution)/shard_map/reduce_scatter | solution.py:113
  522.0 0.8 broadcast_multiply_fusion
  522.9 4.6 copy.59
  527.5 0.7 convolution_convert_fusion
  528.2 0.5 reshape_reshape.11
  528.8 114.1 %reduce-scatter.5.cloned.1.call-done = bf16[16,2048]{1,0:T(8,128)(2,1)} async-done(((bf16[512,2048]{1,0:T(8,128)(2,1)}), bf16[16,2048]{1,0:T(8,128)(2,1)}) %reduce-scatter.5.cloned.1.call-update) | async-done | bytes 65552 | tf_op jit(solution)/shard_map/reduce_scatter | solution.py:103
  642.9 1.8 fusion.2
  (52 shorter events, 4.5 us)
Async XLA Ops:
  7.4 408.8 %copy-start = (bf16[342,2048]{1,0:T(8,128)(2,1)S(1)}, bf16[342,2048]{1,0:T(8,128)(2,1)}, u32[]{:S(2)}) copy-start(bf16[342,2048]{1,0:T(8,128)(2,1)} %param.19) | copy-start | bytes 4202500
  7.4 96.5 %copy-start.2 = (bf16[4,16,342]{2,1,0:T(8,128)(2,1)S(1)}, bf16[4,16,342]{2,1,0:T(8,128)(2,1)}, u32[]{:S(2)}) copy-start(bf16[4,16,342]{2,1,0:T(8,128)(2,1)} %param.21) | copy-start | bytes 131332
  7.4 233.1 %all-gather.3.cloned.1.call-start = ((), (), s32[]{:S(2)}) async-start(), calls=%async_computation.2 | async-start | bytes 2162688 | tf_op jit(solution)/shard_map/all_gather | solution.py:76
  10.7 511.3 %reduce-scatter.7.cloned.1.call-start = ((), (), s32[]{:S(2)}) async-start(), calls=%async_computation.5 | async-start | bytes 135168 | tf_op jit(solution)/shard_map/reduce_scatter | solution.py:113
  103.5 42.3 %copy-start.3 = (bf16[4,16,342]{2,1,0:T(8,128)(2,1)S(1)}, bf16[4,16,342]{2,1,0:T(8,128)(2,1)}, u32[]{:S(2)}) copy-start(bf16[4,16,342]{2,1,0:T(8,128)(2,1)} %param.23) | copy-start | bytes 131332
  145.4 46.7 %copy-start.4 = (bf16[4,342,16]{1,2,0:T(8,128)(2,1)S(1)}, bf16[4,342,16]{1,2,0:T(8,128)(2,1)}, u32[]{:S(2)}) copy-start(bf16[4,342,16]{1,2,0:T(8,128)(2,1)} %param.24) | copy-start | bytes 131332
  238.0 2.2 copy-start.7
  238.0 2.3 copy-start.6
  240.2 169.6 %copy-start.8 = (bf16[2048,342]{0,1:T(8,128)(2,1)S(1)}, bf16[2048,342]{0,1:T(8,128)(2,1)}, u32[]{:S(2)}) copy-start(bf16[2048,342]{0,1:T(8,128)(2,1)} %param.17) | copy-start | bytes 4202500
  409.8 3.0 copy-start.5
  409.9 3.0 copy-start.9
  412.9 0.9 copy-start.1
  415.3 107.6 %all-gather.5.cloned.1.call-start = ((), (), s32[]{:S(2)}) async-start(), calls=%async_computation.4 | async-start | bytes 4456448 | tf_op jit(solution)/shard_map/all_gather | solution.py:53
  415.9 227.0 %reduce-scatter.5.cloned.1.call-start = ((), (), s32[]{:S(2)}) async-start(), calls=%async_computation.3 | async-start | bytes 2162688 | tf_op jit(solution)/shard_map/reduce_scatter | solution.py:103
Sparse Core Ops, SparseCore 0:
  11.3 83.0 all-gather.2
  415.4 106.5 reduce-scatter.6
  526.4 116.4 reduce-scatter.4
Sparse Core Ops, SparseCore 1:
  417.9 92.9 all-gather.4
where the time goes:
time: 652 us
  blocking collectives  385 us (59%)
  waiting for transfers between devices  218 us (33%)
  between operations  14.9 us (2%)
  local copies, waits for them, and re-layouts  14.7 us (2%)
  matrix products  12.5 us (2%)
  other arithmetic  6.66 us (1%)
    psum x1, blocking collectives, local(): mids = lax.psum(partial_mid.astype(jnp.bfloat16), 'tensor')  168 us
    reduce_scatter x1, waiting for transfers between devices, local(): lax.psum_scatter(jnp.dot(hidden, w_down, preferred_element_type=jnp.float...  114 us
    reduce_scatter x1, waiting for transfers between devices, local(): lax.psum_scatter(partial_down.astype(jnp.bfloat16), 'tensor', scatter_dim...  103 us
    all_gather x1, blocking collectives, local(): lax.all_gather(up_a, 'seq', axis=0, tiled=True)  44.6 us
    all_gather x1, blocking collectives, local(): lax.all_gather(up_b, 'seq', axis=0, tiled=True)  44.4 us
    all_gather x1, blocking collectives, local(): lax.all_gather(gate_a, 'seq', axis=0, tiled=True)  44.3 us
    all_gather x1, blocking collectives, local(): lax.all_gather(down_a, 'seq', axis=0, tiled=True)  43.4 us
    all_gather x1, blocking collectives, local(): lax.all_gather(gate_b, 'seq', axis=0, tiled=True)  40.5 us
  transfers between devices with their start and end apart: 4, of which 2 were waited for; matrix products, arithmetic and copies ran while one was open for 3% of the time, Pallas kernels for 0%

commit v1 on v0

--- a/solution.py
+++ b/solution.py
@@ -45,7 +45,9 @@
     matches = used_adapters[:, None] == jnp.arange(adapters_n, dtype=jnp.int32)[None, :]
     slot_used = jnp.sum(jnp.where(matches, adapter_holder[None, :], 0), axis=1)
     whole = (
-        lax.all_gather(gate_a, "seq", axis=0, tiled=True),
+        jnp.concatenate(
+            lax.all_to_all(jnp.stack([gate_a] * lax.axis_size("seq")), "seq", 0, 0), axis=0
+        ),
         lax.all_gather(up_a, "seq", axis=0, tiled=True),
         lax.all_gather(gate_b, "seq", axis=0, tiled=True),
         lax.all_gather(up_b, "seq", axis=0, tiled=True),

time: 652 us -> 627 us (0.962)
  blocking collectives: 385 us -> 349 us
  starting transfers between devices: 0.31 us -> 9.81 us
    all_gather x1 -> x0, blocking collectives: 44.3 us -> none  [local(): lax.all_gather(gate_a, 'seq', axis=0, tiled=True)]
    all_gather x1, blocking collectives: 40.5 us -> 50.5 us  [local(): lax.all_gather(gate_b, 'seq', axis=0, tiled=True)]
    all_to_all x0 -> x1, starting transfers between devices: none -> 9.68 us  [local(): lax.all_to_all(jnp.stack([gate_a] * lax.axis_size('seq')), 'seq', 0, 0)]
  transfers between devices with their start and end apart: 4 -> 5, of which waited for: 2 -> 2; matrix products, arithmetic and copies ran while one was open for 3% -> 5% of each run, Pallas kernels for 0% -> 0%
where the time goes in v1:
time: 627 us; the launch traced here: 626 us
  blocking collectives  349 us (56%)
  waiting for transfers between devices  212 us (34%)
  local copies, waits for them, and re-layouts  21 us (3%)
  matrix products  15.3 us (2%)
  between operations  14.9 us (2%)
  starting transfers between devices  9.81 us (2%)
    psum x1, blocking collectives, local(): mids = lax.psum(partial_mid.astype(jnp.bfloat16), 'tensor')  172 us
    reduce_scatter x1, waiting for transfers between devices, local(): lax.psum_scatter(jnp.dot(hidden, w_down, preferred_element_type=jnp.float...  114 us
    reduce_scatter x1, waiting for transfers between devices, local(): lax.psum_scatter(partial_down.astype(jnp.bfloat16), 'tensor', scatter_dim...  97.3 us
    all_gather x1, blocking collectives, local(): lax.all_gather(gate_b, 'seq', axis=0, tiled=True)  50.5 us
    all_gather x1, blocking collectives, local(): lax.all_gather(down_a, 'seq', axis=0, tiled=True)  45.4 us
    all_gather x1, blocking collectives, local(): lax.all_gather(up_b, 'seq', axis=0, tiled=True)  41.7 us
    all_gather x1, blocking collectives, local(): lax.all_gather(up_a, 'seq', axis=0, tiled=True)  39.7 us
  transfers between devices with their start and end apart: 5, of which 2 were waited for; matrix products, arithmetic and copies ran while one was open for 5% of the time, Pallas kernels for 0%

profile of v1, /device:TPU:8, one launch (start us, length us, event | category | flops | bytes accessed | tf_op | source)
XLA Modules:
  0.0 626.5 jit_solution(15860333317958537191)
XLA Ops:
  7.4 1.1 fusion.10
  8.5 0.7 convert_element_type.78
  9.2 1.5 fusion.12
  10.7 0.8 broadcast_bitcast_fusion
  11.5 0.9 reshape.174
  12.4 9.7 %all-to-all-start = ((bf16[16,2,2048]{2,1,0:T(2,128)(2,1)}), bf16[16,2,2048]{2,1,0:T(2,128)(2,1)}, u32[]{:S(2)}, u32[]{:S(2)}) async-start(bf16[16,2,2048]{2,1,0:T(2,128)(2,1)} %reshape.174), calls=%async_computation | async-start | bytes 262144 | tf_op jit(solution)/shard_map/all_to_all | solution.py:49
  22.1 39.7 %all_gather.19 = bf16[64,64,16]{1,2,0:T(8,128)(2,1)S(1)} all-gather(bf16[4,64,16]{1,2,0:T(8,128)(2,1)} %param.22), channel_id=1, replica_groups=mesh['tensor'=32,'seq'=16] {'seq'}, dimensions={0}, use_global_device_ids=true | all-gather | bytes 139264 | tf_op jit(solution)/shard_map/all_gather | solution.py:51
  61.9 1.1 copy.50
  62.9 50.5 %all_gather.20 = bf16[64,16,342]{2,1,0:T(8,128)(2,1)S(1)} all-gather(bf16[4,16,342]{2,1,0:T(8,128)(2,1)} %param.21), channel_id=1, replica_groups=mesh['tensor'=32,'seq'=16] {'seq'}, dimensions={0}, use_global_device_ids=true | all-gather | bytes 744192 | tf_op jit(solution)/shard_map/all_gather | solution.py:52
  113.4 0.7 reshape.164
  114.2 41.7 %all_gather.21 = bf16[64,16,342]{2,1,0:T(8,128)(2,1)S(1)} all-gather(bf16[4,16,342]{2,1,0:T(8,128)(2,1)S(1)} %copy-done.3), channel_id=1, replica_groups=mesh['tensor'=32,'seq'=16] {'seq'}, dimensions={0}, use_global_device_ids=true | all-gather | bytes 744192 | tf_op jit(solution)/shard_map/all_gather | solution.py:53
  155.9 1.6 reshape.165
  157.5 45.4 %all_gather.22 = bf16[64,342,16]{1,2,0:T(8,128)(2,1)} all-gather(bf16[4,342,16]{1,2,0:T(8,128)(2,1)S(1)} %copy-done.4), channel_id=1, replica_groups=mesh['tensor'=32,'seq'=16] {'seq'}, dimensions={0}, use_global_device_ids=true | all-gather | bytes 744192 | tf_op jit(solution)/shard_map/all_gather | solution.py:54
  202.9 2.4 copy.54
  205.6 1.0 convolution_convert_fusion.3
  206.6 1.4 convolution_convert_fusion.2
  208.0 1.2 convolution_convert_fusion.1
  210.6 1.9 reshape.167
  213.4 1.1 reshape.175
  215.0 1.8 reshape_reshape.12
  217.4 1.3 fusion.13
  218.8 171.6 %psum.7 = bf16[512,2,16]{0,2,1:T(8,128)(2,1)S(1)} all-reduce(bf16[512,2,16]{0,2,1:T(8,128)(2,1)S(1)} %multiply_reduce_fusion), channel_id=1, replica_groups=mesh['tensor'=32,'seq'=16] {'tensor'}, use_global_device_ids=true, to_apply=%region_6.7 | all-reduce | flops 16384 | bytes 65536 | tf_op jit(solution)/shard_map/psum | solution.py:87
  390.4 3.1 fusion.28
  393.8 0.9 fusion.29
  395.4 0.8 copy.58
  396.9 2.6 convolution_convert_fusion.4
  399.7 97.3 %reduce-scatter.7.cloned.1.call-done = bf16[16,16]{1,0:T(8,128)(2,1)} async-done(((bf16[512,16]{1,0:T(8,128)(2,1)}), bf16[16,16]{1,0:T(8,128)(2,1)}) %reduce-scatter.7.cloned.1.call-update) | async-done | bytes 528 | tf_op jit(solution)/shard_map/reduce_scatter | solution.py:115
  497.0 0.8 broadcast_multiply_fusion
  497.9 4.6 copy.60
  502.5 0.7 convolution_convert_fusion
  503.7 113.8 %reduce-scatter.5.cloned.1.call-done = bf16[16,2048]{1,0:T(8,128)(2,1)} async-done(((bf16[512,2048]{1,0:T(8,128)(2,1)}), bf16[16,2048]{1,0:T(8,128)(2,1)}) %reduce-scatter.5.cloned.1.call-update) | async-done | bytes 65552 | tf_op jit(solution)/shard_map/reduce_scatter | solution.py:105
  617.6 1.8 fusion.2
  (59 shorter events, 6.2 us)
Async XLA Ops:
  7.4 389.5 %copy-start = (bf16[342,2048]{1,0:T(8,128)(2,1)S(1)}, bf16[342,2048]{1,0:T(8,128)(2,1)}, u32[]{:S(2)}) copy-start(bf16[342,2048]{1,0:T(8,128)(2,1)} %param.19) | copy-start | bytes 4202500
  7.4 210.0 %all-gather.3.cloned.1.call-start = ((), (), s32[]{:S(2)}) async-start(), calls=%async_computation.3 | async-start | bytes 2162688 | tf_op jit(solution)/shard_map/all_gather | solution.py:78
  10.7 103.5 %copy-start.3 = (bf16[4,16,342]{2,1,0:T(8,128)(2,1)S(1)}, bf16[4,16,342]{2,1,0:T(8,128)(2,1)}, u32[]{:S(2)}) copy-start(bf16[4,16,342]{2,1,0:T(8,128)(2,1)} %param.23) | copy-start | bytes 131332
  12.4 201.0 %all-to-all-start = ((bf16[16,2,2048]{2,1,0:T(2,128)(2,1)}), bf16[16,2,2048]{2,1,0:T(2,128)(2,1)}, u32[]{:S(2)}, u32[]{:S(2)}) async-start(bf16[16,2,2048]{2,1,0:T(2,128)(2,1)} %reshape.174), calls=%async_computation | async-start | bytes 262144 | tf_op jit(solution)/shard_map/all_to_all | solution.py:49
  22.1 474.9 %reduce-scatter.7.cloned.1.call-start = ((), (), s32[]{:S(2)}) async-start(), calls=%async_computation.6 | async-start | bytes 135168 | tf_op jit(solution)/shard_map/reduce_scatter | solution.py:115
  113.4 44.1 %copy-start.4 = (bf16[4,342,16]{1,2,0:T(8,128)(2,1)S(1)}, bf16[4,342,16]{1,2,0:T(8,128)(2,1)}, u32[]{:S(2)}) copy-start(bf16[4,342,16]{1,2,0:T(8,128)(2,1)} %param.24) | copy-start | bytes 131332
  155.9 49.5 %copy-start.8 = (s32[64]{0:T(128)S(1)}, s32[64]{0:T(128)}, u32[]{:S(2)}) copy-start(s32[64]{0:T(128)} %param.29) | copy-start | bytes 772
  155.9 49.5 %copy-start.9 = (s32[16]{0:T(128)S(1)}, s32[16]{0:T(128)}, u32[]{:S(2)}) copy-start(s32[16]{0:T(128)} %param.28) | copy-start | bytes 196
  205.4 3.8 copy-start.1
  205.4 4.0 copy-start.10
  206.6 3.4 copy-start.2
  209.8 3.5 copy-start.6
  390.4 3.4 copy-start.5
  390.4 3.4 copy-start.7
  396.2 101.7 %all-gather.5.cloned.1.call-start = ((), (), s32[]{:S(2)}) async-start(), calls=%async_computation.5 | async-start | bytes 4456448 | tf_op jit(solution)/shard_map/all_gather | solution.py:55
  396.8 220.8 %reduce-scatter.5.cloned.1.call-start = ((), (), s32[]{:S(2)}) async-start(), calls=%async_computation.4 | async-start | bytes 2162688 | tf_op jit(solution)/shard_map/reduce_scatter | solution.py:105
Sparse Core Ops, SparseCore 0:
  11.3 83.0 all-gather.2
  396.3 100.5 reduce-scatter.6
  501.4 116.1 reduce-scatter.4
Sparse Core Ops, SparseCore 1:
  398.8 86.3 all-gather.4
